TPU v7x, 128 devices: a whole 4x4x4 slice. The times are simulated.
128 devices in a mesh: ra: 16 (over z, y), dec: 8 (over x, core).
Axes of the slice: x: 4, y: 4, z: 4, core: 2. Of those that a mesh axis runs over, the one named last changes fastest.
Arguments:
- features: bfloat16 [512, 256, 128], P('ra', 'dec'), may hold values from -6 to 6
- conv_weight: bfloat16 [3, 3, 128, 128], replicated, may hold values from -0.1875 to 0.1875
- conv_bias: float32 [128], replicated, may hold values from -3 to 3
- corners: int32 [16, 8, 200, 2], P('ra', 'dec'), may hold values from 0 to 25
- owner_ids: int32 [16, 8, 200, 1], P('ra', 'dec'), may hold values from 0 to 127; in each aligned block of 200 rows (0 to 199, 200 to 399, ..., all dimensions but the last counted through in order) at most 3 rows name the same one
- labels: int32 [16, 8, 200], P('ra', 'dec'), may hold values from 0 to 2
- head_w1: bfloat16 [128, 6272, 512], P(('ra', 'dec')), may hold values from -0.078125 to 0.078125
- head_b1: float32 [128, 512], P(('ra', 'dec')), may hold values from -3 to 3
- head_w2: bfloat16 [128, 512, 3], P(('ra', 'dec')), may hold values from -1 to 1
- head_b2: float32 [128, 3], P(('ra', 'dec')), may hold values from -4 to 4
Outputs:
- grad_features: bfloat16 [512, 256, 128], P('ra', 'dec')
- grad_conv: float32 [3, 3, 128, 128], replicated
- grad_w1: bfloat16 [128, 6272, 512], P(('ra', 'dec'))
Inputs may be any that keep to these rules, and one draw needn't show every extreme that they name: `corners`: every crop lies inside its own tile. `owner_ids`: at most 3 objects of one tile go to one expert, and every expert gets some object.
All inputs are finite; a program needn't handle non-finite values.
Results may differ from a plain program's by a relative error of at most 0.0095.
Values may be sent and summed in bfloat16 or wider, within the bound.
No kernel may reach another device: no remote copies, remote signals or barrier semaphores. Data moves between devices by JAX's collectives and lax.ppermute only.
A program may use at most 128 MiB of HBM per device.

v0:
```python
import jax
import jax.numpy as jnp
from jax import lax
from jax.sharding import PartitionSpec as P

CROP = 7
loss_scale = 8.0


def padded_2(cells, sides, width):
    for axis, dim in sides:
        count = lax.axis_size(axis)
        ends = count - 1
        head = lax.slice_in_dim(cells, 0, width, axis=dim)
        tail = lax.slice_in_dim(cells, cells.shape[dim] - width, cells.shape[dim], axis=dim)
        cells = jnp.concatenate(
            [
                lax.ppermute(tail, axis, [(i, (i + 1) % count) for i in range(ends)]),
                cells,
                lax.ppermute(head, axis, [((i + 1) % count, i) for i in range(ends)]),
            ],
            axis=dim,
        )
    return cells


def silu_slope(value):
    logistic = jax.nn.sigmoid(value)
    return logistic * (1.0 + value * (1.0 - logistic))


def rank_in_owner(owner_list, owners_all):
    onehot = (owner_list[:, None] == jnp.arange(owners_all, dtype=jnp.int32)[None, :]).astype(
        jnp.int32
    )
    running = jnp.cumsum(onehot, axis=0)
    return jnp.sum(running * onehot, axis=1) - 1


def head_pass(crop_rows, target_rows, weight_one, bias_one, weight_two, bias_two):
    hid_pre = jnp.dot(crop_rows, weight_one, preferred_element_type=jnp.float32) + bias_one[None, :]
    hidden = jax.nn.silu(hid_pre).astype(jnp.bfloat16)
    logits = jnp.dot(hidden, weight_two, preferred_element_type=jnp.float32) + bias_two[None, :]
    target = target_rows.astype(jnp.float32)
    live_float = jnp.sum(target, axis=1, keepdims=True)
    dlogit = (loss_scale * (live_float * jax.nn.sigmoid(logits) - target)).astype(jnp.bfloat16)
    hid_grad = lax.dot_general(
        dlogit, weight_two, (((1,), (1,)), ((), ())), preferred_element_type=jnp.float32
    )
    hid_grad = (hid_grad * silu_slope(hid_pre)).astype(jnp.bfloat16)
    grad_one = lax.dot_general(
        crop_rows, hid_grad, (((0,), (0,)), ((), ())), preferred_element_type=jnp.float32
    )
    crop_grad = lax.dot_general(
        hid_grad, weight_one, (((1,), (1,)), ((), ())), preferred_element_type=jnp.float32
    )
    return (grad_one.astype(jnp.bfloat16), crop_grad.astype(jnp.bfloat16))


def local(
    features, conv_weight, conv_bias, corners, owner_ids, labels, head_w1, head_b1, head_w2, head_b2
):
    tile_rows, tile_cols, channels = features.shape
    padded = padded_2(features, (("ra", 0), ("dec", 1)), 1)
    pre_conv = jnp.zeros((tile_rows * tile_cols, channels), jnp.float32)
    for row_off in range(3):
        for col_off in range(3):
            window = padded[row_off : row_off + tile_rows, col_off : col_off + tile_cols].reshape(
                -1, channels
            )
            pre_conv = pre_conv + jnp.dot(
                window, conv_weight[row_off, col_off], preferred_element_type=jnp.float32
            )
    pre_conv = (pre_conv + conv_bias[None, :]).reshape(tile_rows, tile_cols, channels)
    activation = jax.nn.silu(pre_conv).astype(jnp.bfloat16)
    count_ra = lax.axis_size("ra")
    count_dec = lax.axis_size("dec")
    owners_all = count_ra * count_dec
    owner_list = owner_ids.reshape(-1)
    corner_list = corners.reshape(-1, 2)
    object_count = owner_list.shape[0]
    capacity = (object_count + owners_all - 1) // owners_all + 1
    slot_total = owners_all * capacity
    classes = head_w2.shape[2]
    crop_size = CROP * CROP * channels
    slot_rank = rank_in_owner(owner_list, owners_all)
    slot_index = owner_list * capacity + slot_rank
    offsets = jnp.arange(CROP, dtype=jnp.int32)
    row_index = corner_list[:, 0][:, None, None] + offsets[None, :, None]
    col_index = corner_list[:, 1][:, None, None] + offsets[None, None, :]
    crop_rows = activation[row_index, col_index].reshape(object_count, crop_size)
    onehot_label = (
        labels.reshape(-1)[:, None] == jnp.arange(classes, dtype=jnp.int32)[None, :]
    ).astype(jnp.bfloat16)
    slot_object = (
        jnp.full((slot_total,), -1, jnp.int32)
        .at[slot_index]
        .set(jnp.arange(object_count, dtype=jnp.int32))
    )
    slot_live = slot_object >= 0
    slot_safe = jnp.where(slot_live, slot_object, 0)
    send_rows = jnp.where(
        slot_live[:, None], jnp.take(crop_rows, slot_safe, axis=0), jnp.zeros((), jnp.bfloat16)
    )
    send_target = jnp.where(
        slot_live[:, None], jnp.take(onehot_label, slot_safe, axis=0), jnp.zeros((), jnp.bfloat16)
    )
    weight_one = head_w1[0]
    bias_one = head_b1[0]
    weight_two = head_w2[0]
    bias_two = head_b2[0]
    got_rows, got_target = (
        lax.all_to_all(
            send_rows.reshape(owners_all, capacity, crop_size),
            ("ra", "dec"),
            split_axis=0,
            concat_axis=0,
            tiled=True,
        ),
        lax.all_to_all(
            send_target.reshape(owners_all, capacity, classes),
            ("ra", "dec"),
            split_axis=0,
            concat_axis=0,
            tiled=True,
        ),
    )
    grad_one, crop_grad = head_pass(
        got_rows.reshape(-1, crop_size),
        got_target.reshape(-1, classes),
        weight_one,
        bias_one,
        weight_two,
        bias_two,
    )
    returned = lax.all_to_all(
        crop_grad.reshape(owners_all, capacity, crop_size),
        ("ra", "dec"),
        split_axis=0,
        concat_axis=0,
        tiled=True,
    )
    back_rows = jnp.take(returned.reshape(-1, crop_size), slot_index, axis=0)
    values = back_rows.reshape(object_count, CROP, CROP, channels).astype(jnp.float32)
    act_grad = (
        jnp.zeros((tile_rows, tile_cols, channels), jnp.float32)
        .at[row_index, col_index]
        .add(values)
    )
    pre_grad = (act_grad * silu_slope(pre_conv)).astype(jnp.bfloat16)
    grad_padded = padded_2(pre_grad, (("ra", 0), ("dec", 1)), 1)
    pre_flat = pre_grad.reshape(-1, channels)
    tap_list = []
    grad_feat = jnp.zeros((tile_rows * tile_cols, channels), jnp.float32)
    for row_off in range(3):
        for col_off in range(3):
            window = padded[row_off : row_off + tile_rows, col_off : col_off + tile_cols].reshape(
                -1, channels
            )
            tap_list.append(
                lax.dot_general(
                    window, pre_flat, (((0,), (0,)), ((), ())), preferred_element_type=jnp.float32
                )
            )
            shifted = grad_padded[
                2 - row_off : 2 - row_off + tile_rows, 2 - col_off : 2 - col_off + tile_cols
            ].reshape(-1, channels)
            grad_feat = grad_feat + lax.dot_general(
                shifted,
                conv_weight[row_off, col_off],
                (((1,), (1,)), ((), ())),
                preferred_element_type=jnp.float32,
            )
    local_taps = jnp.stack(tap_list).reshape(3, 3, channels, channels)
    grad_conv = lax.psum(local_taps, ("ra", "dec"))
    grad_features = grad_feat.reshape(tile_rows, tile_cols, channels).astype(jnp.bfloat16)
    return (grad_features, grad_conv, grad_one[None])


def solution(mesh):
    in_specs = (
        P("ra", "dec", None),
        P(),
        P(),
        P("ra", "dec", None, None),
        P("ra", "dec", None, None),
        P("ra", "dec", None),
        P(("ra", "dec"), None, None),
        P(("ra", "dec"), None),
        P(("ra", "dec"), None, None),
        P(("ra", "dec"), None),
    )
    out_specs = (P("ra", "dec", None), P(), P(("ra", "dec"), None, None))
    return jax.shard_map(local, mesh=mesh, in_specs=in_specs, out_specs=out_specs, check_vma=False)
```

profile of v0, /device:TPU:1, one launch (start us, length us, event | category | flops | bytes accessed | tf_op | source)
XLA Modules:
  0.0 652.4 jit_solution(923496613759407383)
XLA Ops:
  7.2 0.8 iota_compare_fusion.1
  8.3 0.9 fusion.48
  9.1 0.7 compare_select_fusion.2
  9.8 1.2 scatter_custom_fusion
  11.1 0.8 fusion.49
  11.9 1.4 gather_fusion
  14.2 0.7 copy.30
  14.9 11.5 %all-to-all-start = ((bf16[128,3,3]{1,2,0:T(4,128)(2,1)}), bf16[128,3,3]{1,2,0:T(4,128)(2,1)S(1)}, u32[]{:S(2)}, u32[]{:S(2)}) async-start(bf16[128,3,3]{1,2,0:T(4,128)(2,1)} %copy.30), calls=%async_computation | async-start | bytes 262144 | tf_op jit(solution)/shard_map/all_to_all | solution.py:120
  26.4 0.7 fusion.106
  27.2 3.3 collective-permute-start
  30.4 1.3 collective-permute-start.1
  31.7 0.8 fusion.107
  33.5 1.1 constant_dynamic-update-slice_fusion.3
  34.7 0.5 collective-permute-done.1
  35.2 4.5 collective-permute-start.2
  39.7 2.1 collective-permute-start.3
  42.3 2.4 collective-permute-done.3
  46.9 107.8 %gather_fusion.1 = bf16[9800,128]{1,0:T(8,128)(2,1)} fusion(bf16[32,32,128]{2,1,0:T(8,128)(2,1)S(1)} %multiply_convert_fusion.4, s32[9800]{0:T(1024)S(1)} %reshape.291), kind=kCustom, calls=%fused_computation.1 | custom fusion | bytes 5096000 | tf_op jit(solution)/shard_map/gather | solution.py:91
  154.6 4.5 reshape.263
  159.2 5.8 gather_fusion.2
  165.0 11.5 %gather.25 = bf16[128,3,6272]{2,1,0:T(4,128)(2,1)} reshape(bf16[384,6272]{1,0:T(8,128)(2,1)} %gather_fusion.2) | data formatting | bytes 9633792 | tf_op jit(solution)/shard_map/jit(_take)/gather | solution.py:103
  176.4 9.0 %select_select_fusion = bf16[128,3,6272]{2,1,0:T(4,128)(2,1)} fusion(bf16[128,3,6272]{2,1,0:T(4,128)(2,1)} %gather.25, pred[128,3]{1,0:T(8,128)(4,1)S(1)} %broadcast_in_dim.103, pred[128,3]{1,0:T(8,128)(4,1)S(1)} %broadcast_in_dim.101), kind=kLoop, calls=%fused_computation.12 | loop fusion | flops 4816896 | bytes 9634560 | tf_op jit(solution)/shard_map/jit(_where)/select_n | solution.py:102
  185.4 11.1 %all-to-all-start.1 = ((bf16[128,3,6272]{2,1,0:T(4,128)(2,1)}), bf16[128,3,6272]{2,1,0:T(4,128)(2,1)}, u32[]{:S(2)}, u32[]{:S(2)}) async-start(bf16[128,3,6272]{2,1,0:T(4,128)(2,1)} %select_select_fusion), calls=%async_computation.1 | async-start | bytes 12845056 | tf_op jit(solution)/shard_map/all_to_all | solution.py:113
  197.2 76.0 %all-to-all-done.1 = bf16[128,3,6272]{2,1,0:T(4,128)(2,1)} async-done(((bf16[128,3,6272]{2,1,0:T(4,128)(2,1)}), bf16[128,3,6272]{2,1,0:T(4,128)(2,1)}, u32[]{:S(2)}, u32[]{:S(2)}) %all-to-all-start.1) | async-done | bytes 4816928 | tf_op jit(solution)/shard_map/all_to_all | solution.py:113
  273.2 12.4 %reshape.264 = bf16[384,6272]{1,0:T(8,128)(2,1)} reshape(bf16[128,3,6272]{2,1,0:T(4,128)(2,1)} %all-to-all-done.1) | data formatting | bytes 9633792 | tf_op jit(solution)/shard_map/reshape | solution.py:129
  285.6 6.3 fusion.4
  292.0 0.8 fusion.7
  292.7 8.7 %convolution_convert_fusion.1 = bf16[384,6272]{1,0:T(8,128)(2,1)} fusion(bf16[384,512]{1,0:T(8,128)(2,1)S(1)} %fusion.7, bf16[1,6272,512]{2,1,0:T(8,128)(2,1)} %param.16), kind=kOutput, calls=%fused_computation.7 | convolution fusion | flops 2468659200 | bytes 11632640 | tf_op jit(solution)/shard_map/dot_general | solution.py:54
  301.5 11.5 %reshape.265 = bf16[128,3,6272]{2,1,0:T(4,128)(2,1)} reshape(bf16[384,6272]{1,0:T(8,128)(2,1)} %convolution_convert_fusion.1) | data formatting | bytes 9633792 | tf_op jit(solution)/shard_map/reshape | solution.py:137
  313.0 6.5 %all-to-all-start.2 = ((bf16[128,3,6272]{2,1,0:T(4,128)(2,1)}), bf16[128,3,6272]{2,1,0:T(4,128)(2,1)}, u32[]{:S(2)}, u32[]{:S(2)}) async-start(bf16[128,3,6272]{2,1,0:T(4,128)(2,1)} %reshape.265), calls=%async_computation.2 | async-start | bytes 12845056 | tf_op jit(solution)/shard_map/all_to_all | solution.py:136
  321.0 7.8 %fusion = bf16[1,6272,512]{2,1,0:T(8,128)(2,1)} fusion(bf16[384,6272]{1,0:T(8,128)(2,1)} %reshape.264, bf16[384,512]{1,0:T(8,128)(2,1)S(1)} %fusion.7), kind=kOutput, calls=%fused_computation.8 | convolution fusion | flops 2469462016 | bytes 11632640 | tf_op jit(solution)/shard_map/dot_general | solution.py:51
  328.8 67.3 %all-to-all-done.2 = bf16[128,3,6272]{2,1,0:T(4,128)(2,1)} async-done(((bf16[128,3,6272]{2,1,0:T(4,128)(2,1)}), bf16[128,3,6272]{2,1,0:T(4,128)(2,1)}, u32[]{:S(2)}, u32[]{:S(2)}) %all-to-all-start.2) | async-done | bytes 4816928 | tf_op jit(solution)/shard_map/all_to_all | solution.py:136
  396.1 12.4 %reshape.266 = bf16[384,6272]{1,0:T(8,128)(2,1)} reshape(bf16[128,3,6272]{2,1,0:T(4,128)(2,1)} %all-to-all-done.2) | data formatting | bytes 9633792 | tf_op jit(solution)/shard_map/reshape | solution.py:143
  408.6 8.9 %gather_fusion.3 = bf16[200,6272]{1,0:T(8,128)(2,1)} fusion(bf16[384,6272]{1,0:T(8,128)(2,1)} %reshape.266, s32[1024]{0:T(1024)S(1)} %pad_clamp_fusion), kind=kCustom, calls=%fused_computation.3 | custom fusion | bytes 5018400 | tf_op jit(solution)/shard_map/jit(_take)/gather | solution.py:143
  417.5 5.2 gather.27
  422.6 3.0 select_convert_fusion
  425.6 6.7 %reshape.323 = f32[9800,128]{1,0:T(8,128)} reshape(f32[200,7,7,128]{3,2,1,0:T(8,128)} %select_convert_fusion) | data formatting | bytes 10035200 | tf_op jit(solution)/shard_map/convert_element_type | solution.py:144
  432.3 55.8 %scatter_custom_fusion.1 = f32[1024,128]{1,0:T(8,128)S(1)} fusion(s32[9800]{0:T(1024)S(1)} %reshape.321, f32[9800,128]{1,0:T(8,128)} %reshape.323, f32[]{:T(128)} %constant.27.clone.1), kind=kCustom, calls=%fused_computation.90 | custom fusion | flops 1254400 | bytes 524800
  488.6 1.3 collective-permute-start.5
  489.9 4.0 collective-permute-start.4
  493.9 1.2 fusion.14
  497.2 0.8 copy-done.20
  498.1 3.3 collective-permute-start.6
  501.4 3.4 collective-permute-start.7
  505.1 0.6 collective-permute-done.7
  507.8 0.9 fusion.12
  508.7 135.0 %all-reduce.3.cloned.1.call-done = f32[3,3,128,128]{3,2,1,0:T(8,128)} async-done(((f32[3,3,128,128]{3,2,1,0:T(8,128)}), f32[3,3,128,128]{3,2,1,0:T(8,128)}) %all-reduce.3.cloned.1.call-update) | async-done | bytes 589840 | tf_op jit(solution)/shard_map/psum | solution.py:175
  643.7 1.9 copy.52
  (136 shorter events, 11.3 us)
Async XLA Ops:
  7.2 284.8 %copy-start = (bf16[1,512,3]{1,2,0:T(4,128)(2,1)S(1)}, bf16[1,512,3]{1,2,0:T(4,128)(2,1)}, u32[]{:S(2)}) copy-start(bf16[1,512,3]{1,2,0:T(4,128)(2,1)} %param.18) | copy-start | bytes 9220
  7.2 34.7 %copy-start.4 = (bf16[3,3,128,128]{3,2,1,0:T(8,128)(2,1)S(1)}, bf16[3,3,128,128]{3,2,1,0:T(8,128)(2,1)}, u32[]{:S(2)}) copy-start(bf16[3,3,128,128]{3,2,1,0:T(8,128)(2,1)} %param.11) | copy-start | bytes 884740
  14.9 170.5 %all-to-all-start = ((bf16[128,3,3]{1,2,0:T(4,128)(2,1)}), bf16[128,3,3]{1,2,0:T(4,128)(2,1)S(1)}, u32[]{:S(2)}, u32[]{:S(2)}) async-start(bf16[128,3,3]{1,2,0:T(4,128)(2,1)} %copy.30), calls=%async_computation | async-start | bytes 262144 | tf_op jit(solution)/shard_map/all_to_all | solution.py:120
  27.2 6.4 collective-permute-start
  30.4 4.7 collective-permute-start.1
  33.1 12.9 %copy-start.2 = (bf16[32,32,128]{2,1,0:T(8,128)(2,1)S(1)}, bf16[32,32,128]{2,1,0:T(8,128)(2,1)}, u32[]{:S(2)}) copy-start(bf16[32,32,128]{2,1,0:T(8,128)(2,1)} %param.10) | copy-start | bytes 786436
  34.7 7.6 %copy-start.21 = (bf16[33,32,128]{2,1,0:T(8,128)(2,1)}, bf16[33,32,128]{2,1,0:T(8,128)(2,1)S(1)}, u32[]{:S(2)}) copy-start(bf16[33,32,128]{2,1,0:T(8,128)(2,1)S(1)} %get-tuple-element.28) | copy-start | bytes 811012
  35.1 6.7 %copy-start.18 = (bf16[33,32,128]{2,1,0:T(8,128)(2,1)}, bf16[33,32,128]{2,1,0:T(8,128)(2,1)S(1)}, u32[]{:S(2)}) copy-start(bf16[33,32,128]{2,1,0:T(8,128)(2,1)S(1)} %get-tuple-element.35) | copy-start | bytes 811012
  35.2 7.1 %collective-permute-start.2 = (bf16[34,1,128]{2,1,0:T(2,128)(2,1)S(1)}, bf16[34,1,128]{2,1,0:T(2,128)(2,1)S(1)}, u32[]{:S(2)}, u32[]{:S(2)}) collective-permute-start(bf16[34,1,128]{2,1,0:T(2,128)(2,1)S(1)} %get-tuple-element.22), channel_id=1, source_target_pairs={{0,1},{1,2},{2,3},{3,4},{4,5},{5,6},{6,7},{8,9},{9,10},{10,11},{11... | collective-permute-start | bytes 26120 | tf_op jit(solution)/shard_map/ppermute | solution.py:18
  39.7 5.1 collective-permute-start.3
  41.8 4.7 copy-start.24
  45.1 1.2 copy-start.6
  45.1 1.6 copy-start.12
  45.1 1.6 copy-start.14
  45.1 1.6 copy-start.16
  45.1 1.8 copy-start.8
  45.1 1.8 copy-start.10
  185.4 87.7 %all-to-all-start.1 = ((bf16[128,3,6272]{2,1,0:T(4,128)(2,1)}), bf16[128,3,6272]{2,1,0:T(4,128)(2,1)}, u32[]{:S(2)}, u32[]{:S(2)}) async-start(bf16[128,3,6272]{2,1,0:T(4,128)(2,1)} %select_select_fusion), calls=%async_computation.1 | async-start | bytes 12845056 | tf_op jit(solution)/shard_map/all_to_all | solution.py:113
  196.8 88.8 %copy-start.25 = (f32[1,512]{1,0:T(1,128)S(1)}, f32[1,512]{1,0:T(1,128)}, u32[]{:S(2)}) copy-start(f32[1,512]{1,0:T(1,128)} %param.17) | copy-start | bytes 6148
  285.6 6.4 copy-start.26
  313.0 6.9 %copy-start.23 = (s32[2]{0:T(128)S(1)}, s32[2]{0:T(128)}, u32[]{:S(2)}) copy-start(s32[2]{0:T(128)} %constant.87) | copy-start | bytes 28
  313.0 8.0 %copy-start.22 = (s32[1,1,200,1]{2,3,1,0:T(1,128)S(1)}, s32[1,1,200,1]{2,3,1,0:T(1,128)}, u32[]{:S(2)}) copy-start(s32[1,1,200,1]{2,3,1,0:T(1,128)} %param.14) | copy-start | bytes 2404
  313.0 83.2 %all-to-all-start.2 = ((bf16[128,3,6272]{2,1,0:T(4,128)(2,1)}), bf16[128,3,6272]{2,1,0:T(4,128)(2,1)}, u32[]{:S(2)}, u32[]{:S(2)}) async-start(bf16[128,3,6272]{2,1,0:T(4,128)(2,1)} %reshape.265), calls=%async_computation.2 | async-start | bytes 12845056 | tf_op jit(solution)/shard_map/all_to_all | solution.py:136
  319.5 324.1 %all-reduce.3.cloned.1.call-start = ((), (), s32[]{:S(2)}) async-start(), calls=%async_computation.3 | async-start | bytes 1179648 | tf_op jit(solution)/shard_map/psum | solution.py:175
  425.6 62.7 %copy-start.15 = (bf16[32,32,128]{2,1,0:T(8,128)(2,1)S(1)}, bf16[32,32,128]{2,1,0:T(8,128)(2,1)}, u32[]{:S(2)}) copy-start(bf16[32,32,128]{2,1,0:T(8,128)(2,1)} %copy-done.14) | copy-start | bytes 786436
  425.6 69.5 %copy-start.13 = (bf16[32,32,128]{2,1,0:T(8,128)(2,1)S(1)}, bf16[32,32,128]{2,1,0:T(8,128)(2,1)}, u32[]{:S(2)}) copy-start(bf16[32,32,128]{2,1,0:T(8,128)(2,1)} %copy-done.12) | copy-start | bytes 786436
  425.6 69.8 %copy-start.11 = (bf16[32,32,128]{2,1,0:T(8,128)(2,1)S(1)}, bf16[32,32,128]{2,1,0:T(8,128)(2,1)}, u32[]{:S(2)}) copy-start(bf16[32,32,128]{2,1,0:T(8,128)(2,1)} %copy-done.10) | copy-start | bytes 786436
  425.6 70.1 %copy-start.3 = (bf16[32,32,128]{2,1,0:T(8,128)(2,1)S(1)}, bf16[32,32,128]{2,1,0:T(8,128)(2,1)}, u32[]{:S(2)}) copy-start(bf16[32,32,128]{2,1,0:T(8,128)(2,1)} %param.10) | copy-start | bytes 786436
  432.3 63.7 %copy-start.9 = (bf16[32,32,128]{2,1,0:T(8,128)(2,1)S(1)}, bf16[32,32,128]{2,1,0:T(8,128)(2,1)}, u32[]{:S(2)}) copy-start(bf16[32,32,128]{2,1,0:T(8,128)(2,1)} %copy-done.8) | copy-start | bytes 786436
  432.3 64.6 %copy-start.7 = (bf16[32,32,128]{2,1,0:T(8,128)(2,1)S(1)}, bf16[32,32,128]{2,1,0:T(8,128)(2,1)}, u32[]{:S(2)}) copy-start(bf16[32,32,128]{2,1,0:T(8,128)(2,1)} %copy-done.6) | copy-start | bytes 786436
  488.1 8.2 %copy-start.17 = (bf16[32,32,128]{2,1,0:T(8,128)(2,1)S(1)}, bf16[32,32,128]{2,1,0:T(8,128)(2,1)}, u32[]{:S(2)}) copy-start(bf16[32,32,128]{2,1,0:T(8,128)(2,1)} %copy-done.16) | copy-start | bytes 786436
  488.1 8.5 %copy-start.19 = (bf16[33,32,128]{2,1,0:T(8,128)(2,1)S(1)}, bf16[33,32,128]{2,1,0:T(8,128)(2,1)}, u32[]{:S(2)}) copy-start(bf16[33,32,128]{2,1,0:T(8,128)(2,1)} %copy-done.18) | copy-start | bytes 811012
  488.1 16.7 %copy-start.5 = (bf16[3,3,128,128]{3,2,1,0:T(8,128)(2,1)S(1)}, bf16[3,3,128,128]{3,2,1,0:T(8,128)(2,1)}, u32[]{:S(2)}) copy-start(bf16[3,3,128,128]{3,2,1,0:T(8,128)(2,1)} %param.11) | copy-start | bytes 884740
  488.6 9.4 %collective-permute-start.5 = (bf16[1,32,128]{2,1,0:T(8,128)(2,1)S(1)}, bf16[1,32,128]{2,1,0:T(8,128)(2,1)S(1)}, u32[]{:S(2)}, u32[]{:S(2)}) collective-permute-start(bf16[1,32,128]{2,1,0:T(8,128)(2,1)S(1)} %get-tuple-element.27), channel_id=1, source_target_pairs={{8,0},{16,8},{24,16},{32,24},{40,32},{48,40},{56,48},{64,56},{72,6... | collective-permute-start | bytes 24584 | tf_op jit(solution)/shard_map/ppermute | solution.py:20
  489.9 8.1 %collective-permute-start.4 = (bf16[1,32,128]{2,1,0:T(8,128)(2,1)S(1)}, bf16[1,32,128]{2,1,0:T(8,128)(2,1)S(1)}, u32[]{:S(2)}, u32[]{:S(2)}) collective-permute-start(bf16[1,32,128]{2,1,0:T(8,128)(2,1)S(1)} %get-tuple-element.26), channel_id=1, source_target_pairs={{0,8},{8,16},{16,24},{24,32},{32,40},{40,48},{48,56},{56,64},{64,7... | collective-permute-start | bytes 24584 | tf_op jit(solution)/shard_map/ppermute | solution.py:18
  497.2 0.8 copy-start.20
  498.1 7.0 %collective-permute-start.6 = (bf16[34,1,128]{2,1,0:T(2,128)(2,1)S(1)}, bf16[34,1,128]{2,1,0:T(2,128)(2,1)S(1)}, u32[]{:S(2)}, u32[]{:S(2)}) collective-permute-start(bf16[34,1,128]{2,1,0:T(2,128)(2,1)S(1)} %get-tuple-element.17), channel_id=1, source_target_pairs={{1,0},{2,1},{3,2},{4,3},{5,4},{6,5},{7,6},{9,8},{10,9},{11,10},{12... | collective-permute-start | bytes 26120 | tf_op jit(solution)/shard_map/ppermute | solution.py:20
  501.4 4.3 collective-permute-start.7
  506.1 139.5 %copy-start.1 = (bf16[1,512,3]{1,2,0:T(4,128)(2,1)S(1)}, bf16[1,512,3]{1,2,0:T(4,128)(2,1)}, u32[]{:S(2)}) copy-start(bf16[1,512,3]{1,2,0:T(4,128)(2,1)} %param.18) | copy-start | bytes 9220
Sparse Core Ops, SparseCore 0:
  498.1 145.4 all-reduce.2
where the time goes:
time: 655 us; the launch traced here: 652 us
  waiting for transfers between devices  282 us (43%)
  local copies, waits for them, and re-layouts  199 us (30%)
  other arithmetic  73.1 us (11%)
  starting transfers between devices  52.3 us (8%)
  matrix products  31.7 us (5%)
  between operations  15 us (2%)
    psum x1, waiting for transfers between devices, local(): grad_conv = lax.psum(local_taps, ('ra', 'dec'))  135 us
    gather x1, local copies, waits for them, and re-layouts, local(): activation[row_index, col_index].reshape(object_count, crop_size)  108 us
    all_to_all x1, waiting for transfers between devices, local(): lax.all_to_all(send_rows.reshape(owners_all, capacity, crop_size), ('ra',...  76 us
    all_to_all x1, waiting for transfers between devices, local(): lax.all_to_all(crop_grad.reshape(owners_all, capacity, crop_size), ('ra',...  67.3 us
    unnamed x4, other arithmetic  56.2 us
    gather x2, local copies, waits for them, and re-layouts, local(): jnp.take(crop_rows, slot_safe, axis=0)  17.2 us
    ppermute x4, starting transfers between devices, padded_2(): lax.ppermute(tail, axis, [(i, (i + 1) % count) for i in range(ends)])  15.1 us
    gather x2, local copies, waits for them, and re-layouts, local(): back_rows = jnp.take(returned.reshape(-1, crop_size), slot_index, axis=0)  14.1 us
  transfers between devices with their start and end apart: 12, of which 6 were waited for; matrix products, arithmetic and copies ran while one was open for 25% of the time, Pallas kernels for 0%

commit v1 on v0

--- a/solution.py
+++ b/solution.py
@@ -5,6 +5,10 @@
 
 CROP = 7
 loss_scale = 8.0
+
+
+def keep_up_task(z, shard_axis):
+    return jnp.sum(lax.all_gather(z, shard_axis), 0)
 
 
 def padded_2(cells, sides, width):
@@ -172,7 +176,7 @@
                 preferred_element_type=jnp.float32,
             )
     local_taps = jnp.stack(tap_list).reshape(3, 3, channels, channels)
-    grad_conv = lax.psum(local_taps, ("ra", "dec"))
+    grad_conv = keep_up_task(local_taps, ("ra", "dec"))
     grad_features = grad_feat.reshape(tile_rows, tile_cols, channels).astype(jnp.bfloat16)
     return (grad_features, grad_conv, grad_one[None])
 

time: 655 us -> 718 us (1.096)
  waiting for transfers between devices: 282 us -> 307 us
  other arithmetic: 73.1 us -> 97.1 us
  starting transfers between devices: 52.3 us -> 63.3 us
    all_gather x0 -> x1, waiting for transfers between devices: none -> 153 us  [keep_up_task(): return jnp.sum(lax.all_gather(z, shard_axis), 0)]
    psum x1 -> x0, waiting for transfers between devices: 135 us -> none  [local(): grad_conv = lax.psum(local_taps, ('ra', 'dec'))]
    reduce_sum x0 -> x1, other arithmetic: none -> 24.1 us  [keep_up_task(): return jnp.sum(lax.all_gather(z, shard_axis), 0)]
    all_to_all x1, starting transfers between devices: 11.1 us -> 21.6 us  [local(): lax.all_to_all(send_rows.reshape(owners_all, capacity, crop_size), ('ra',...]
    all_to_all x1, waiting for transfers between devices: 67.3 us -> 75.2 us  [local(): lax.all_to_all(crop_grad.reshape(owners_all, capacity, crop_size), ('ra',...]
  transfers between devices with their start and end apart: 12 -> 12, of which waited for: 6 -> 6; matrix products, arithmetic and copies ran while one was open for 25% -> 22% of each run, Pallas kernels for 0% -> 0%
where the time goes in v1:
time: 718 us; the launch traced here: 712 us
  waiting for transfers between devices  307 us (43%)
  local copies, waits for them, and re-layouts  197 us (27%)
  other arithmetic  97.1 us (14%)
  starting transfers between devices  63.3 us (9%)
  matrix products  32.7 us (5%)
  between operations  15.2 us (2%)
    all_gather x1, waiting for transfers between devices, keep_up_task(): return jnp.sum(lax.all_gather(z, shard_axis), 0)  153 us
    gather x1, local copies, waits for them, and re-layouts, local(): activation[row_index, col_index].reshape(object_count, crop_size)  108 us
    all_to_all x1, waiting for transfers between devices, local(): lax.all_to_all(send_rows.reshape(owners_all, capacity, crop_size), ('ra',...  76 us
    all_to_all x1, waiting for transfers between devices, local(): lax.all_to_all(crop_grad.reshape(owners_all, capacity, crop_size), ('ra',...  75.2 us
    unnamed x4, other arithmetic  56.2 us
    reduce_sum x1, other arithmetic, keep_up_task(): return jnp.sum(lax.all_gather(z, shard_axis), 0)  24.1 us
    all_to_all x1, starting transfers between devices, local(): lax.all_to_all(send_rows.reshape(owners_all, capacity, crop_size), ('ra',...  21.6 us
    gather x2, local copies, waits for them, and re-layouts, local(): jnp.take(crop_rows, slot_safe, axis=0)  17.2 us
  transfers between devices with their start and end apart: 12, of which 6 were waited for; matrix products, arithmetic and copies ran while one was open for 22% of the time, Pallas kernels for 0%

profile of v1, /device:TPU:1, one launch (start us, length us, event | category | flops | bytes accessed | tf_op | source)
XLA Modules:
  0.0 712.1 jit_solution(11535418767573319517)
XLA Ops:
  7.2 0.8 iota_compare_fusion.1
  8.3 0.9 fusion.48
  9.1 0.7 compare_select_fusion.2
  9.8 1.2 scatter_custom_fusion
  11.1 0.8 fusion.49
  11.9 1.4 gather_fusion
  14.2 0.8 copy.30
  14.9 11.5 %all-to-all-start = ((bf16[128,3,3]{1,2,0:T(4,128)(2,1)}), bf16[128,3,3]{1,2,0:T(4,128)(2,1)S(1)}, u32[]{:S(2)}, u32[]{:S(2)}) async-start(bf16[128,3,3]{1,2,0:T(4,128)(2,1)} %copy.30), calls=%async_computation | async-start | bytes 262144 | tf_op jit(solution)/shard_map/all_to_all | solution.py:124
  26.4 0.7 fusion.106
  27.2 3.3 collective-permute-start
  30.5 1.3 collective-permute-start.1
  31.8 0.8 fusion.107
  33.6 1.1 constant_dynamic-update-slice_fusion.3
  34.7 0.5 collective-permute-done.1
  35.2 4.5 collective-permute-start.2
  39.7 2.3 collective-permute-start.3
  42.5 2.2 collective-permute-done.3
  46.9 107.8 %gather_fusion.1 = bf16[9800,128]{1,0:T(8,128)(2,1)} fusion(bf16[32,32,128]{2,1,0:T(8,128)(2,1)S(1)} %multiply_convert_fusion.4, s32[9800]{0:T(1024)S(1)} %reshape.287), kind=kCustom, calls=%fused_computation.1 | custom fusion | bytes 5096000 | tf_op jit(solution)/shard_map/gather | solution.py:95
  154.6 4.5 reshape.260
  159.2 5.8 gather_fusion.2
  165.0 11.5 %gather.25 = bf16[128,3,6272]{2,1,0:T(4,128)(2,1)} reshape(bf16[384,6272]{1,0:T(8,128)(2,1)} %gather_fusion.2) | data formatting | bytes 9633792 | tf_op jit(solution)/shard_map/jit(_take)/gather | solution.py:107
  176.4 9.0 %select_select_fusion = bf16[128,3,6272]{2,1,0:T(4,128)(2,1)} fusion(bf16[128,3,6272]{2,1,0:T(4,128)(2,1)} %gather.25, pred[128,3]{1,0:T(8,128)(4,1)S(1)} %broadcast_in_dim.103, pred[128,3]{1,0:T(8,128)(4,1)S(1)} %broadcast_in_dim.101), kind=kLoop, calls=%fused_computation.12 | loop fusion | flops 4816896 | bytes 9634560 | tf_op jit(solution)/shard_map/jit(_where)/select_n | solution.py:106
  185.4 21.6 %all-to-all-start.1 = ((bf16[128,3,6272]{2,1,0:T(4,128)(2,1)}), bf16[128,3,6272]{2,1,0:T(4,128)(2,1)}, u32[]{:S(2)}, u32[]{:S(2)}) async-start(bf16[128,3,6272]{2,1,0:T(4,128)(2,1)} %select_select_fusion), calls=%async_computation.1 | async-start | bytes 12845056 | tf_op jit(solution)/shard_map/all_to_all | solution.py:117
  207.7 76.0 %all-to-all-done.1 = bf16[128,3,6272]{2,1,0:T(4,128)(2,1)} async-done(((bf16[128,3,6272]{2,1,0:T(4,128)(2,1)}), bf16[128,3,6272]{2,1,0:T(4,128)(2,1)}, u32[]{:S(2)}, u32[]{:S(2)}) %all-to-all-start.1) | async-done | bytes 4816928 | tf_op jit(solution)/shard_map/all_to_all | solution.py:117
  283.6 12.5 %reshape.261 = bf16[384,6272]{1,0:T(8,128)(2,1)} reshape(bf16[128,3,6272]{2,1,0:T(4,128)(2,1)} %all-to-all-done.1) | data formatting | bytes 9633792 | tf_op jit(solution)/shard_map/reshape | solution.py:133
  296.1 6.3 fusion.4
  302.5 0.8 fusion.7
  303.3 8.9 %convolution_convert_fusion.1 = bf16[384,6272]{1,0:T(8,128)(2,1)} fusion(bf16[384,512]{1,0:T(8,128)(2,1)S(1)} %fusion.7, bf16[1,6272,512]{2,1,0:T(8,128)(2,1)} %param.16), kind=kOutput, calls=%fused_computation.7 | convolution fusion | flops 2468659200 | bytes 11632640 | tf_op jit(solution)/shard_map/dot_general | solution.py:58
  312.2 11.5 %reshape.262 = bf16[128,3,6272]{2,1,0:T(4,128)(2,1)} reshape(bf16[384,6272]{1,0:T(8,128)(2,1)} %convolution_convert_fusion.1) | data formatting | bytes 9633792 | tf_op jit(solution)/shard_map/reshape | solution.py:141
  323.7 6.4 all-to-all-start.2
  331.5 75.2 %all-to-all-done.2 = bf16[128,3,6272]{2,1,0:T(4,128)(2,1)} async-done(((bf16[128,3,6272]{2,1,0:T(4,128)(2,1)}), bf16[128,3,6272]{2,1,0:T(4,128)(2,1)}, u32[]{:S(2)}, u32[]{:S(2)}) %all-to-all-start.2) | async-done | bytes 4816928 | tf_op jit(solution)/shard_map/all_to_all | solution.py:140
  406.7 12.4 %reshape.263 = bf16[384,6272]{1,0:T(8,128)(2,1)} reshape(bf16[128,3,6272]{2,1,0:T(4,128)(2,1)} %all-to-all-done.2) | data formatting | bytes 9633792 | tf_op jit(solution)/shard_map/reshape | solution.py:147
  419.1 8.9 %gather_fusion.3 = bf16[200,6272]{1,0:T(8,128)(2,1)} fusion(bf16[384,6272]{1,0:T(8,128)(2,1)} %reshape.263, s32[1024]{0:T(1024)S(1)} %pad_clamp_fusion), kind=kCustom, calls=%fused_computation.3 | custom fusion | bytes 5018400 | tf_op jit(solution)/shard_map/jit(_take)/gather | solution.py:147
  428.0 5.2 gather.27
  433.2 3.0 select_convert_fusion
  436.2 6.7 reshape.319
  442.9 55.7 %scatter_custom_fusion.1 = f32[1024,128]{1,0:T(8,128)S(1)} fusion(s32[9800]{0:T(1024)S(1)} %reshape.317, f32[9800,128]{1,0:T(8,128)} %reshape.319, f32[]{:T(128)} %constant.27.clone.1), kind=kCustom, calls=%fused_computation.90 | custom fusion | flops 1254400 | bytes 524800
  499.1 1.2 fusion.14
  502.4 0.8 copy-done.20
  503.2 1.3 collective-permute-start.5
  504.5 4.1 collective-permute-start.4
  508.6 8.7 %fusion = bf16[1,6272,512]{2,1,0:T(8,128)(2,1)} fusion(bf16[384,6272]{1,0:T(8,128)(2,1)} %reshape.261, bf16[384,512]{1,0:T(8,128)(2,1)} %copy-done.27), kind=kOutput, calls=%fused_computation.8 | convolution fusion | flops 2469462016 | bytes 11632640 | tf_op jit(solution)/shard_map/dot_general | solution.py:55
  517.4 3.6 collective-permute-start.6
  521.0 3.5 collective-permute-start.7
  524.8 0.6 collective-permute-done.7
  527.4 0.9 fusion.12
  528.4 152.6 %all-gather.2.cloned.1.call-done = f32[128,3,3,128,128]{4,3,2,1,0:T(8,128)} async-done(((f32[1,3,3,128,128]{4,3,2,1,0:T(8,128)}), f32[128,3,3,128,128]{4,3,2,1,0:T(8,128)}) %all-gather.2.cloned.1.call-update) | async-done | bytes 75497488 | tf_op jit(solution)/shard_map/all_gather | solution.py:11
  681.0 24.1 %reduce_sum.29 = f32[3,3,128,128]{3,2,1,0:T(8,128)} reduce(f32[128,3,3,128,128]{4,3,2,1,0:T(8,128)} %all-gather.2.cloned.1.call-done, f32[]{:T(128)} %constant.27.clone.1), dimensions={0}, to_apply=%region_6.7 | reduce | flops 18726912 | bytes 76087296 | tf_op jit(solution)/shard_map/reduce_sum | solution.py:11
  (138 shorter events, 11.3 us)
Async XLA Ops:
  7.2 295.3 %copy-start = (bf16[1,512,3]{1,2,0:T(4,128)(2,1)S(1)}, bf16[1,512,3]{1,2,0:T(4,128)(2,1)}, u32[]{:S(2)}) copy-start(bf16[1,512,3]{1,2,0:T(4,128)(2,1)} %param.18) | copy-start | bytes 9220
  7.2 34.9 %copy-start.4 = (bf16[3,3,128,128]{3,2,1,0:T(8,128)(2,1)S(1)}, bf16[3,3,128,128]{3,2,1,0:T(8,128)(2,1)}, u32[]{:S(2)}) copy-start(bf16[3,3,128,128]{3,2,1,0:T(8,128)(2,1)} %param.11) | copy-start | bytes 884740
  14.9 170.5 %all-to-all-start = ((bf16[128,3,3]{1,2,0:T(4,128)(2,1)}), bf16[128,3,3]{1,2,0:T(4,128)(2,1)S(1)}, u32[]{:S(2)}, u32[]{:S(2)}) async-start(bf16[128,3,3]{1,2,0:T(4,128)(2,1)} %copy.30), calls=%async_computation | async-start | bytes 262144 | tf_op jit(solution)/shard_map/all_to_all | solution.py:124
  27.2 6.4 collective-permute-start
  30.5 4.7 collective-permute-start.1
  33.1 12.9 %copy-start.2 = (bf16[32,32,128]{2,1,0:T(8,128)(2,1)S(1)}, bf16[32,32,128]{2,1,0:T(8,128)(2,1)}, u32[]{:S(2)}) copy-start(bf16[32,32,128]{2,1,0:T(8,128)(2,1)} %param.10) | copy-start | bytes 786436
  34.7 7.8 %copy-start.21 = (bf16[33,32,128]{2,1,0:T(8,128)(2,1)}, bf16[33,32,128]{2,1,0:T(8,128)(2,1)S(1)}, u32[]{:S(2)}) copy-start(bf16[33,32,128]{2,1,0:T(8,128)(2,1)S(1)} %get-tuple-element.28) | copy-start | bytes 811012
  35.2 6.9 copy-start.18
  35.2 7.3 %collective-permute-start.2 = (bf16[34,1,128]{2,1,0:T(2,128)(2,1)S(1)}, bf16[34,1,128]{2,1,0:T(2,128)(2,1)S(1)}, u32[]{:S(2)}, u32[]{:S(2)}) collective-permute-start(bf16[34,1,128]{2,1,0:T(2,128)(2,1)S(1)} %get-tuple-element.22), channel_id=1, source_target_pairs={{0,1},{1,2},{2,3},{3,4},{4,5},{5,6},{6,7},{8,9},{9,10},{10,11},{11... | collective-permute-start | bytes 26120 | tf_op jit(solution)/shard_map/ppermute | solution.py:22
  39.7 5.1 collective-permute-start.3
  42.0 4.5 copy-start.24
  45.1 1.1 copy-start.6
  45.1 1.6 copy-start.12
  45.1 1.6 copy-start.14
  45.1 1.6 copy-start.16
  45.1 1.7 copy-start.8
  45.1 1.7 copy-start.10
  185.4 98.2 %all-to-all-start.1 = ((bf16[128,3,6272]{2,1,0:T(4,128)(2,1)}), bf16[128,3,6272]{2,1,0:T(4,128)(2,1)}, u32[]{:S(2)}, u32[]{:S(2)}) async-start(bf16[128,3,6272]{2,1,0:T(4,128)(2,1)} %select_select_fusion), calls=%async_computation.1 | async-start | bytes 12845056 | tf_op jit(solution)/shard_map/all_to_all | solution.py:117
  207.2 88.9 %copy-start.25 = (f32[1,512]{1,0:T(1,128)S(1)}, f32[1,512]{1,0:T(1,128)}, u32[]{:S(2)}) copy-start(f32[1,512]{1,0:T(1,128)} %param.17) | copy-start | bytes 6148
  296.1 6.4 copy-start.26
  303.3 8.9 %copy-start.27 = (bf16[384,512]{1,0:T(8,128)(2,1)}, bf16[384,512]{1,0:T(8,128)(2,1)S(1)}, u32[]{:S(2)}) copy-start(bf16[384,512]{1,0:T(8,128)(2,1)S(1)} %fusion.7) | copy-start | bytes 1179652
  323.7 6.8 copy-start.23
  323.7 7.8 %copy-start.22 = (s32[1,1,200,1]{2,3,1,0:T(1,128)S(1)}, s32[1,1,200,1]{2,3,1,0:T(1,128)}, u32[]{:S(2)}) copy-start(s32[1,1,200,1]{2,3,1,0:T(1,128)} %param.14) | copy-start | bytes 2404
  323.7 83.0 %all-to-all-start.2 = ((bf16[128,3,6272]{2,1,0:T(4,128)(2,1)}), bf16[128,3,6272]{2,1,0:T(4,128)(2,1)}, u32[]{:S(2)}, u32[]{:S(2)}) async-start(bf16[128,3,6272]{2,1,0:T(4,128)(2,1)} %reshape.262), calls=%async_computation.2 | async-start | bytes 12845056 | tf_op jit(solution)/shard_map/all_to_all | solution.py:140
  330.0 350.9 %all-gather.2.cloned.1.call-start = ((), (), s32[]{:S(2)}) async-start(), calls=%async_computation.3 | async-start | bytes 76087296 | tf_op jit(solution)/shard_map/all_gather | solution.py:11
  436.2 62.7 %copy-start.15 = (bf16[32,32,128]{2,1,0:T(8,128)(2,1)S(1)}, bf16[32,32,128]{2,1,0:T(8,128)(2,1)}, u32[]{:S(2)}) copy-start(bf16[32,32,128]{2,1,0:T(8,128)(2,1)} %copy-done.14) | copy-start | bytes 786436
  436.2 64.2 %copy-start.13 = (bf16[32,32,128]{2,1,0:T(8,128)(2,1)S(1)}, bf16[32,32,128]{2,1,0:T(8,128)(2,1)}, u32[]{:S(2)}) copy-start(bf16[32,32,128]{2,1,0:T(8,128)(2,1)} %copy-done.12) | copy-start | bytes 786436
  436.2 64.5 %copy-start.11 = (bf16[32,32,128]{2,1,0:T(8,128)(2,1)S(1)}, bf16[32,32,128]{2,1,0:T(8,128)(2,1)}, u32[]{:S(2)}) copy-start(bf16[32,32,128]{2,1,0:T(8,128)(2,1)} %copy-done.10) | copy-start | bytes 786436
  436.2 64.7 %copy-start.3 = (bf16[32,32,128]{2,1,0:T(8,128)(2,1)S(1)}, bf16[32,32,128]{2,1,0:T(8,128)(2,1)}, u32[]{:S(2)}) copy-start(bf16[32,32,128]{2,1,0:T(8,128)(2,1)} %param.10) | copy-start | bytes 786436
  442.9 58.3 %copy-start.9 = (bf16[32,32,128]{2,1,0:T(8,128)(2,1)S(1)}, bf16[32,32,128]{2,1,0:T(8,128)(2,1)}, u32[]{:S(2)}) copy-start(bf16[32,32,128]{2,1,0:T(8,128)(2,1)} %copy-done.8) | copy-start | bytes 786436
  442.9 58.6 %copy-start.17 = (bf16[32,32,128]{2,1,0:T(8,128)(2,1)S(1)}, bf16[32,32,128]{2,1,0:T(8,128)(2,1)}, u32[]{:S(2)}) copy-start(bf16[32,32,128]{2,1,0:T(8,128)(2,1)} %copy-done.16) | copy-start | bytes 786436
  442.9 59.2 %copy-start.7 = (bf16[32,32,128]{2,1,0:T(8,128)(2,1)S(1)}, bf16[32,32,128]{2,1,0:T(8,128)(2,1)}, u32[]{:S(2)}) copy-start(bf16[32,32,128]{2,1,0:T(8,128)(2,1)} %copy-done.6) | copy-start | bytes 786436
  498.6 3.2 copy-start.19
  502.3 0.8 copy-start.20
  503.2 14.2 %collective-permute-start.5 = (bf16[1,32,128]{2,1,0:T(8,128)(2,1)S(1)}, bf16[1,32,128]{2,1,0:T(8,128)(2,1)S(1)}, u32[]{:S(2)}, u32[]{:S(2)}) collective-permute-start(bf16[1,32,128]{2,1,0:T(8,128)(2,1)S(1)} %get-tuple-element.27), channel_id=1, source_target_pairs={{8,0},{16,8},{24,16},{32,24},{40,32},{48,40},{56,48},{64,56},{72,6... | collective-permute-start | bytes 24584 | tf_op jit(solution)/shard_map/ppermute | solution.py:24
  504.5 20.0 %copy-start.5 = (bf16[3,3,128,128]{3,2,1,0:T(8,128)(2,1)S(1)}, bf16[3,3,128,128]{3,2,1,0:T(8,128)(2,1)}, u32[]{:S(2)}) copy-start(bf16[3,3,128,128]{3,2,1,0:T(8,128)(2,1)} %param.11) | copy-start | bytes 884740
  504.5 12.9 %collective-permute-start.4 = (bf16[1,32,128]{2,1,0:T(8,128)(2,1)S(1)}, bf16[1,32,128]{2,1,0:T(8,128)(2,1)S(1)}, u32[]{:S(2)}, u32[]{:S(2)}) collective-permute-start(bf16[1,32,128]{2,1,0:T(8,128)(2,1)S(1)} %get-tuple-element.26), channel_id=1, source_target_pairs={{0,8},{8,16},{16,24},{24,32},{32,40},{40,48},{48,56},{56,64},{64,7... | collective-permute-start | bytes 24584 | tf_op jit(solution)/shard_map/ppermute | solution.py:22
  517.4 7.4 %collective-permute-start.6 = (bf16[34,1,128]{2,1,0:T(2,128)(2,1)S(1)}, bf16[34,1,128]{2,1,0:T(2,128)(2,1)S(1)}, u32[]{:S(2)}, u32[]{:S(2)}) collective-permute-start(bf16[34,1,128]{2,1,0:T(2,128)(2,1)S(1)} %get-tuple-element.17), channel_id=1, source_target_pairs={{1,0},{2,1},{3,2},{4,3},{5,4},{6,5},{7,6},{9,8},{10,9},{11,10},{12... | collective-permute-start | bytes 26120 | tf_op jit(solution)/shard_map/ppermute | solution.py:24
  521.0 4.4 collective-permute-start.7
  681.0 24.1 %copy-start.1 = (bf16[1,512,3]{1,2,0:T(4,128)(2,1)S(1)}, bf16[1,512,3]{1,2,0:T(4,128)(2,1)}, u32[]{:S(2)}) copy-start(bf16[1,512,3]{1,2,0:T(4,128)(2,1)} %param.18) | copy-start | bytes 9220
Sparse Core Ops, SparseCore 0:
  503.3 177.6 all-gather.1
